TPU v7x, 32 devices: a whole 2x2x4 slice. The times are simulated.
32 devices in a mesh: row: 4 (over z), col: 8 (over y, x, core).
Axes of the slice: x: 2, y: 2, z: 4, core: 2. Of those that a mesh axis runs over, the one named last changes fastest.
Arguments:
- factor_rows: float32 [2, 1024, 4096], P(None, 'col', 'row'), as said below
- adjoint_rows: float32 [2, 1024, 4096], P(None, 'col', 'row'), as said below
- panel_inverse: float32 [2, 1024, 1024], replicated, as said below
Outputs:
- kernel_adjoint: float32 [2, 1024, 4096], P(None, 'col', 'row')
Inputs may be any that keep to these rules, and one draw needn't show every extreme that they name: `factor_rows`: zero right of the diagonal; in panel p the columns J_p hold a lower-triangular block with diagonal entries from 0.5 to 4. `adjoint_rows`: zero right of the diagonal of the same rows. panel_inverse[p] is the inverse of factor_rows[p, :, J_p] to float32 rounding.
All inputs are finite; a program needn't handle non-finite values.
Results may differ from a plain program's by a relative error of at most 0.0001.
Values sent between devices are 32-bit elements; how exact they have to be, the bound alone decides.
No kernel may reach another device: no remote copies, remote signals or barrier semaphores. Data moves between devices by JAX's collectives and lax.ppermute only.
A program may use at most 128 MiB of HBM per device.

v0:
```python
import jax
import jax.numpy as jnp
from jax import lax
from jax.sharding import PartitionSpec as P

HIGHEST = lax.Precision.HIGHEST


def spread(value, axis, source):
    kept = jnp.where(lax.axis_index(axis) == source, value, 0).astype(value.dtype)
    return lax.psum(kept, axis)


def phi_lower(matrix):
    unit_diag = jnp.eye(matrix.shape[0], dtype=jnp.float32)
    return jnp.tril(matrix) * (1.0 - 0.5 * unit_diag)


def product(left_mat, right_mat):
    return jnp.dot(left_mat, right_mat, precision=HIGHEST, preferred_element_type=jnp.float32)


def diag_fix(factor, diag_pre, inverse):
    inner = phi_lower(product(factor.T, diag_pre))
    return phi_lower(product(product(inverse.T, inner + inner.T), inverse))


def fixed_block(factor, diag_term, inverse):
    diag_pre = jnp.tril(lax.psum(diag_term, "col"))
    return diag_fix(factor, diag_pre, inverse)


def local(factor_rows, adjoint_rows, panel_inverse):
    row_count = lax.axis_size("row")
    panels = panel_inverse.shape[0]
    panel_width = panel_inverse.shape[1]
    slab_rows = factor_rows.shape[1]
    span_cols = factor_rows.shape[2]
    row_pos = lax.axis_index("row")
    col_pos = lax.axis_index("col")
    first_col = (row_count - panels) * panel_width
    columns = row_pos * span_cols + jnp.arange(span_cols, dtype=jnp.int32)
    offset = col_pos * slab_rows
    adjoint = adjoint_rows
    for panel in range(panels - 1, -1, -1):
        owner_row = row_count - panels + panel
        is_owner = row_pos == owner_row
        inverse = panel_inverse[panel]
        held_adj, held_fac = (
            spread(adjoint[panel:], "row", owner_row),
            spread(factor_rows[panel:], "row", owner_row),
        )
        col_adjoint = jnp.einsum("qib,bj->qij", held_adj[1:], inverse, precision=HIGHEST)
        placed = lax.dynamic_update_slice(
            jnp.zeros((panel_width, panel_width), jnp.float32), held_adj[0], (offset, 0)
        )
        diag_term = placed - jnp.einsum("qbi,qbj->ij", col_adjoint, held_fac[1:], precision=HIGHEST)
        row_panel = lax.all_gather(factor_rows[panel], "col", axis=0, tiled=True)
        diag_factor = lax.all_gather(held_fac[0], "col", axis=0, tiled=True)
        diag_new = fixed_block(diag_factor, diag_term, inverse)
        sym_rows = lax.dynamic_slice_in_dim(diag_new + diag_new.T, offset, slab_rows, 0)
        left_cols = (columns < first_col + panel * panel_width)[None, :]
        row_update = product(sym_rows, row_panel)
        pieces = [adjoint[:panel]]
        if panel + 1 < panels:
            later_rows = factor_rows[panel + 1 :]
            row_update = (
                lax.psum_scatter(
                    jnp.einsum("qbi,qbj->ij", col_adjoint, later_rows, precision=HIGHEST),
                    "col",
                    scatter_dimension=0,
                    tiled=True,
                )
                + row_update
            )
            block_update = jnp.einsum("qib,bj->qij", col_adjoint, row_panel, precision=HIGHEST)
            lower_new = jnp.where(
                left_cols[None], adjoint[panel + 1 :] - block_update, adjoint[panel + 1 :]
            )
            lower_new = jnp.where(is_owner, col_adjoint, lower_new)
        own_new = jnp.where(left_cols, adjoint[panel] - row_update, adjoint[panel])
        own_new = jnp.where(
            is_owner, lax.dynamic_slice_in_dim(diag_new, offset, slab_rows, 0), own_new
        )
        pieces.append(own_new[None])
        if panel + 1 < panels:
            pieces.append(lower_new)
        adjoint = jnp.concatenate(pieces, axis=0)
    return adjoint


def solution(mesh):
    return jax.shard_map(
        local,
        mesh=mesh,
        in_specs=(P(None, "col", "row"), P(None, "col", "row"), P()),
        out_specs=P(None, "col", "row"),
        check_vma=False,
    )
```

profile of v0, /device:TPU:0, one launch (start us, length us, event | category | flops | bytes accessed | tf_op | source)
XLA Modules:
  0.0 607.5 jit_solution(6495797042716820309)
XLA Ops:
  6.5 1.5 copy.4
  8.1 1.3 fusion.112
  11.5 55.0 %all-reduce.13.cloned.1.call-done = (f32[128,1024]{0,1:T(8,128)}, f32[128,1024]{0,1:T(8,128)}) async-done(((f32[128,1024]{0,1:T(8,128)}, f32[128,1024]{0,1:T(8,128)}), (f32[128,1024]{0,1:T(8,128)}, f32[128,1024]{0,1:T(8,128)})) %all-reduce.13.cloned.1.call-update) | async-done | bytes 1048592 | tf_op jit(solution)/shard_map/psum | solution.py:11
  66.5 2.5 broadcast.53.clone
  71.5 1.3 iota_compare_fusion.1
  73.8 76.7 %all-reduce.7.cloned.1.call-done = f32[1024,1024]{0,1:T(8,128)} async-done(((f32[1024,1024]{0,1:T(8,128)}), f32[1024,1024]{0,1:T(8,128)}) %all-reduce.7.cloned.1.call-update) | async-done | bytes 4194320 | tf_op jit(solution)/shard_map/psum | solution.py:29
  150.6 39.4 %all-gather.8.cloned.1.call-done = f32[1024,1024]{0,1:T(8,128)} async-done(((f32[128,1024]{0,1:T(8,128)}), f32[1024,1024]{0,1:T(8,128)}) %all-gather.8.cloned.1.call-update) | async-done | bytes 4194320 | tf_op jit(solution)/shard_map/all_gather | solution.py:59
  190.0 17.9 %fusion.29 = f32[1024,1024]{1,0:T(8,128)} fusion(f32[1024,1024]{0,1:T(8,128)} %all-gather.8.cloned.1.call-done, f32[1024,1024]{0,1:T(8,128)} %all-reduce.7.cloned.1.call-done), kind=kOutput, calls=%fused_computation.36 | convolution fusion | flops 12886999040 | bytes 12582912 | tf_op jit(solution)/shard_map/dot_general | solution.py:20
  207.8 5.3 copy.8
  213.2 20.0 %fusion.17 = f32[1024,1024]{1,0:T(8,128)S(1)} fusion(f32[1024,1024]{1,0:T(8,128)} %fusion.29, f32[1024,1024]{0,1:T(8,128)} %copy.8, f32[2,1024,1024]{2,1,0:T(8,128)} %param.5), kind=kOutput, calls=%fused_computation.17 | convolution fusion | flops 12898533376 | bytes 16777216 | tf_op jit(solution)/shard_map/dot_general | solution.py:20
  233.2 17.1 %fusion.15 = f32[1024,1024]{1,0:T(8,128)} fusion(f32[1024,1024]{1,0:T(8,128)S(1)} %fusion.17, f32[2,1024,1024]{2,1,0:T(8,128)} %param.5), kind=kOutput, calls=%fused_computation.15 | convolution fusion | flops 12884901888 | bytes 12582912 | tf_op jit(solution)/shard_map/dot_general | solution.py:20
  250.3 5.3 copy.9
  255.7 6.5 %select_multiply_fusion.1 = (f32[1024,1024]{0,1:T(8,128)}, f32[1024,1024]{0,1:T(8,128)}) fusion(f32[1024,1024]{0,1:T(8,128)} %copy.9), kind=kLoop, calls=%fused_computation.28 | loop fusion | flops 9437184 | bytes 12582912 | tf_op jit(solution)/shard_map/mul | solution.py:16
  262.2 6.2 %fusion.50 = f32[128,1024]{0,1:T(8,128)S(1)} fusion(f32[1,1024,1024]{1,2,0:T(8,128)} %all-gather.12.cloned.1.call-done, f32[1024,1024]{0,1:T(8,128)} %bitcast.96, s32[]{:T(128)S(6)} %select_n.105, f32[1024,1024]{0,1:T(8,128)} %get-tuple-element.13, f32[1,128,1024]{1,2,0:T(8,128)S(1)} %copy.23, f32[1024,1024]{0,1:T(8,128)} %get-tuple-element.14, ...), kind=kOutput, calls=%fused_computation.55 | convolution fusion | flops 1611399168 | bytes 7473664 | tf_op jit(solution)/shard_map/dot_general | solution.py:20
  269.5 1.9 slice.43
  271.7 85.6 %all-reduce.11.cloned.1.call-done = (f32[2,128,1024]{1,2,0:T(8,128)}, f32[2,128,1024]{1,2,0:T(8,128)}) async-done(((f32[2,128,1024]{1,2,0:T(8,128)}, f32[2,128,1024]{1,2,0:T(8,128)}), (f32[2,128,1024]{1,2,0:T(8,128)}, f32[2,128,1024]{1,2,0:T(8,128)})) %all-reduce.11.cloned.1.call-update) | async-done | bytes 2097168 | tf_op jit(solution)/shard_map/psum | solution.py:11
  358.5 4.8 fusion.11
  363.3 5.1 convolution_subtract_fusion
  368.5 1.9 slice.44
  370.4 5.0 fusion.89
  375.7 19.2 %all-gather.14.cloned.1.call-done = f32[1,1024,1024]{2,1,0:T(8,128)} async-done(((f32[1,128,1024]{2,1,0:T(8,128)}), f32[1,1024,1024]{2,1,0:T(8,128)}) %all-gather.14.cloned.1.call-update) | async-done | bytes 4194320 | tf_op jit(solution)/shard_map/all_gather | solution.py:58
  394.8 8.7 %fusion.65 = f32[1,128,1024]{1,2,0:T(8,128)S(1)} fusion(f32[128,1024]{0,1:T(8,128)S(1)} %copy.16, f32[128,1024]{0,1:T(8,128)S(1)} %fusion.50, f32[128,1024]{1,0:T(8,128)S(1)} %fusion.11, f32[1,1024,1024]{2,1,0:T(8,128)} %all-gather.14.cloned.1.call-done, pred[1024]{0:T(1024)(128)(4,1)S(1)} %fusion.97, pred[]{:T(512)S(6)} %eq.34), kind=kOutput, calls=%fused_computation.60 | convolution fusion | flops 1611005952 | bytes 6292481 | tf_op jit(solution)/shard_map/qib,bj->qij/dot_general | solution.py:76
  403.5 76.0 %all-reduce.9.cloned.1.call-done = f32[1024,1024]{0,1:T(8,128)} async-done(((f32[1024,1024]{0,1:T(8,128)}), f32[1024,1024]{0,1:T(8,128)}) %all-reduce.9.cloned.1.call-update) | async-done | bytes 4194320 | tf_op jit(solution)/shard_map/psum | solution.py:29
  479.5 39.4 %all-gather.10.cloned.1.call-done = f32[1,1024,1024]{1,2,0:T(8,128)} async-done(((f32[1,128,1024]{1,2,0:T(8,128)}), f32[1,1024,1024]{1,2,0:T(8,128)}) %all-gather.10.cloned.1.call-update) | async-done | bytes 4194320 | tf_op jit(solution)/shard_map/all_gather | solution.py:59
  518.9 17.9 %fusion.22 = f32[1024,1024]{1,0:T(8,128)} fusion(f32[1,1024,1024]{1,2,0:T(8,128)} %all-gather.10.cloned.1.call-done, f32[1024,1024]{0,1:T(8,128)} %all-reduce.9.cloned.1.call-done), kind=kOutput, calls=%fused_computation.22 | convolution fusion | flops 12886999040 | bytes 12582912 | tf_op jit(solution)/shard_map/dot_general | solution.py:20
  536.8 5.3 copy.11
  542.1 20.4 %fusion.6 = f32[1024,1024]{1,0:T(8,128)S(1)} fusion(f32[1024,1024]{1,0:T(8,128)} %fusion.22, f32[1024,1024]{0,1:T(8,128)} %copy.11, f32[2,1024,1024]{2,1,0:T(8,128)} %param.5), kind=kOutput, calls=%fused_computation.7 | convolution fusion | flops 12898533376 | bytes 16777216 | tf_op jit(solution)/shard_map/dot_general | solution.py:20
  562.5 17.0 %fusion.8 = f32[1024,1024]{1,0:T(8,128)} fusion(f32[1024,1024]{1,0:T(8,128)S(1)} %fusion.6, f32[2,1024,1024]{2,1,0:T(8,128)} %param.5), kind=kOutput, calls=%fused_computation.8 | convolution fusion | flops 12884901888 | bytes 12582912 | tf_op jit(solution)/shard_map/dot_general | solution.py:20
  579.5 5.5 copy.12
  585.0 4.7 select_multiply_fusion
  589.7 9.7 %fusion.77 = f32[1,128,1024]{1,2,0:T(8,128)S(1)} fusion(f32[128,1024]{0,1:T(8,128)} %reduce-scatter.2.cloned.1.call-done, f32[1,1024,1024]{2,1,0:T(8,128)} %all-gather.14.cloned.1.call-done, f32[1024,1024]{0,1:T(8,128)} %bitcast.95, s32[]{:T(128)S(6)} %select_n.105, f32[1024,1024]{0,1:T(8,128)} %select_multiply_fusion, f32[1,128,1024]{1,2,0:T(8,128)S(1)} %copy.22, ...), kind=kOutput, calls=%fused_computation.64 | convolution fusion | flops 1611530240 | bytes 7997952 | tf_op jit(solution)/shard_map/dot_general | solution.py:20
  599.5 1.3 copy.17
  (39 shorter events, 8.6 us)
Async XLA Ops:
  6.5 60.0 %all-reduce.13.cloned.1.call-start = ((), (), s32[]{:S(2)}) async-start(), calls=%async_computation.9 | async-start | bytes 2097152 | tf_op jit(solution)/shard_map/psum | solution.py:11
  11.5 139.1 %all-reduce.7.cloned.1.call-start = ((), (), s32[]{:S(2)}) async-start(), calls=%async_computation.2 | async-start | bytes 8388608 | tf_op jit(solution)/shard_map/psum | solution.py:29
  66.5 2.5 copy-start.2
  69.9 120.1 %all-gather.8.cloned.1.call-start = ((), (), s32[]{:S(2)}) async-start(), calls=%async_computation.1 | async-start | bytes 4718592 | tf_op jit(solution)/shard_map/all_gather | solution.py:59
  70.6 191.5 %all-gather.12.cloned.1.call-start = ((), (), s32[]{:S(2)}) async-start(), calls=%async_computation.6 | async-start | bytes 4718592 | tf_op jit(solution)/shard_map/all_gather | solution.py:58
  71.2 286.0 %all-reduce.11.cloned.1.call-start = ((), (), s32[]{:S(2)}) async-start(), calls=%async_computation.8 | async-start | bytes 4194304 | tf_op jit(solution)/shard_map/psum | solution.py:11
  269.5 125.4 %all-gather.14.cloned.1.call-start = ((), (), s32[]{:S(2)}) async-start(), calls=%async_computation.7 | async-start | bytes 4718592 | tf_op jit(solution)/shard_map/all_gather | solution.py:58
  271.4 208.0 %all-reduce.9.cloned.1.call-start = ((), (), s32[]{:S(2)}) async-start(), calls=%async_computation.3 | async-start | bytes 8388608 | tf_op jit(solution)/shard_map/psum | solution.py:29
  357.2 1.2 copy-start.1
  358.4 4.8 copy-start
  368.4 150.5 %all-gather.10.cloned.1.call-start = ((), (), s32[]{:S(2)}) async-start(), calls=%async_computation.5 | async-start | bytes 4718592 | tf_op jit(solution)/shard_map/all_gather | solution.py:59
  370.4 219.3 %reduce-scatter.2.cloned.1.call-start = ((), (), s32[]{:S(2)}) async-start(), calls=%async_computation.4 | async-start | bytes 4718592 | tf_op jit(solution)/shard_map/reduce_scatter | solution.py:68
Sparse Core Ops, SparseCore 0:
  11.6 54.8 all-reduce.12
  70.1 80.3 all-reduce.6
  152.4 37.4 all-gather.7
  191.7 37.4 all-gather.11
  269.6 87.5 all-reduce.10
  359.1 35.6 all-gather.13
  398.5 80.9 all-reduce.8
  481.4 37.4 all-gather.9
  522.3 51.3 reduce-scatter.1
where the time goes:
time: 614 us; the launch traced here: 608 us
  waiting for transfers between devices  393 us (64%)
  matrix products  150 us (24%)
  local copies, waits for them, and re-layouts  34.6 us (6%)
  other arithmetic  16.5 us (3%)
  between operations  13.6 us (2%)
    psum x2, waiting for transfers between devices, fixed_block(): diag_pre = jnp.tril(lax.psum(diag_term, 'col'))  153 us
    psum x2, waiting for transfers between devices, spread(): return lax.psum(kept, axis)  141 us
    dot_general x8, matrix products, product(): jnp.dot(left_mat, right_mat, precision=HIGHEST, preferred_element_type=jn...  126 us
    all_gather x2, waiting for transfers between devices, local(): diag_factor = lax.all_gather(held_fac[0], 'col', axis=0, tiled=True)  78.8 us
    dot_general x4, local copies, waits for them, and re-layouts, product(): jnp.dot(left_mat, right_mat, precision=HIGHEST, preferred_element_type=jn...  21.5 us
    all_gather x2, waiting for transfers between devices, local(): row_panel = lax.all_gather(factor_rows[panel], 'col', axis=0, tiled=True)  19.2 us
  transfers between devices with their start and end apart: 9, of which 7 were waited for; matrix products, arithmetic and copies ran while one was open for 29% of the time, Pallas kernels for 0%

commit v1 on v0

--- a/solution.py
+++ b/solution.py
@@ -56,7 +56,14 @@
         )
         diag_term = placed - jnp.einsum("qbi,qbj->ij", col_adjoint, held_fac[1:], precision=HIGHEST)
         row_panel = lax.all_gather(factor_rows[panel], "col", axis=0, tiled=True)
-        diag_factor = lax.all_gather(held_fac[0], "col", axis=0, tiled=True)
+        ring = [held_fac[0]]
+        for hop in range(7):
+            ring.append(lax.ppermute(ring[-1], "col", [(dev, (dev + 1) % 8) for dev in range(8)]))
+        diag_factor = jnp.roll(
+            jnp.concatenate(ring[::-1], axis=0),
+            (lax.axis_index("col") + 1) * ring[0].shape[0],
+            axis=0,
+        )
         diag_new = fixed_block(diag_factor, diag_term, inverse)
         sym_rows = lax.dynamic_slice_in_dim(diag_new + diag_new.T, offset, slab_rows, 0)
         left_cols = (columns < first_col + panel * panel_width)[None, :]

time: 614 us -> 585 us (0.953)
  waiting for transfers between devices: 393 us -> 337 us
  local copies, waits for them, and re-layouts: 34.6 us -> 58.7 us
    ppermute x0 -> x14, waiting for transfers between devices: none -> 182 us  [local(): lax.ppermute(ring[-1], 'col', [(dev, (dev + 1) % 8) for dev in range(8)])]
    psum x2, waiting for transfers between devices: 153 us -> 15.6 us  [fixed_block(): diag_pre = jnp.tril(lax.psum(diag_term, 'col'))]
    all_gather x2 -> x0, waiting for transfers between devices: 78.8 us -> none  [local(): diag_factor = lax.all_gather(held_fac[0], 'col', axis=0, tiled=True)]
    unnamed x9 -> x57, local copies, waits for them, and re-layouts: 2.64 us -> 25.6 us
    all_gather x2, waiting for transfers between devices: 19.2 us -> 0.02 us  [local(): row_panel = lax.all_gather(factor_rows[panel], 'col', axis=0, tiled=True)]
  transfers between devices with their start and end apart: 9 -> 21, of which waited for: 7 -> 17; matrix products, arithmetic and copies ran while one was open for 29% -> 34% of each run, Pallas kernels for 0% -> 0%
where the time goes in v1:
time: 585 us; the launch traced here: 577 us
  waiting for transfers between devices  337 us (58%)
  matrix products  149 us (25%)
  local copies, waits for them, and re-layouts  58.7 us (10%)
  other arithmetic  16.5 us (3%)
  between operations  14.3 us (2%)
    ppermute x14, waiting for transfers between devices, local(): lax.ppermute(ring[-1], 'col', [(dev, (dev + 1) % 8) for dev in range(8)])  182 us
    psum x2, waiting for transfers between devices, spread(): return lax.psum(kept, axis)  139 us
    dot_general x8, matrix products, product(): jnp.dot(left_mat, right_mat, precision=HIGHEST, preferred_element_type=jn...  126 us
    unnamed x57, local copies, waits for them, and re-layouts  25.6 us
    dot_general x4, local copies, waits for them, and re-layouts, product(): jnp.dot(left_mat, right_mat, precision=HIGHEST, preferred_element_type=jn...  21.7 us
    psum x2, waiting for transfers between devices, fixed_block(): diag_pre = jnp.tril(lax.psum(diag_term, 'col'))  15.6 us
  transfers between devices with their start and end apart: 21, of which 17 were waited for; matrix products, arithmetic and copies ran while one was open for 34% of the time, Pallas kernels for 0%

profile of v1, /device:TPU:0, one launch (start us, length us, event | category | flops | bytes accessed | tf_op | source)
XLA Modules:
  0.0 577.3 jit_solution(16487623730557708800)
XLA Ops:
  11.5 55.0 %all-reduce.13.cloned.1.call-done = (f32[128,1024]{0,1:T(8,128)}, f32[128,1024]{0,1:T(8,128)}) async-done(((f32[128,1024]{0,1:T(8,128)}, f32[128,1024]{0,1:T(8,128)}), (f32[128,1024]{0,1:T(8,128)}, f32[128,1024]{0,1:T(8,128)})) %all-reduce.13.cloned.1.call-update) | async-done | bytes 1048592 | tf_op jit(solution)/shard_map/psum | solution.py:11
  70.7 12.0 %collective-permute-done.7 = f32[128,1024]{0,1:T(8,128)S(1)} collective-permute-done((f32[128,1024]{0,1:T(8,128)S(1)}, f32[128,1024]{0,1:T(8,128)S(1)}, u32[]{:S(2)}, u32[]{:S(2)}) %collective-permute-start.7) | collective-permute-done | bytes 524320 | tf_op jit(solution)/shard_map/ppermute | solution.py:61
  83.2 18.8 %collective-permute-done.8 = f32[128,1024]{0,1:T(8,128)S(1)} collective-permute-done((f32[128,1024]{0,1:T(8,128)S(1)}, f32[128,1024]{0,1:T(8,128)S(1)}, u32[]{:S(2)}, u32[]{:S(2)}) %collective-permute-start.8) | collective-permute-done | bytes 524320 | tf_op jit(solution)/shard_map/ppermute | solution.py:61
  102.8 14.0 %collective-permute-done.9 = f32[128,1024]{0,1:T(8,128)S(1)} collective-permute-done((f32[128,1024]{0,1:T(8,128)S(1)}, f32[128,1024]{0,1:T(8,128)S(1)}, u32[]{:S(2)}, u32[]{:S(2)}) %collective-permute-start.9) | collective-permute-done | bytes 524320 | tf_op jit(solution)/shard_map/ppermute | solution.py:61
  117.6 9.6 %collective-permute-done.10 = f32[128,1024]{0,1:T(8,128)S(1)} collective-permute-done((f32[128,1024]{0,1:T(8,128)S(1)}, f32[128,1024]{0,1:T(8,128)S(1)}, u32[]{:S(2)}, u32[]{:S(2)}) %collective-permute-start.10) | collective-permute-done | bytes 524320 | tf_op jit(solution)/shard_map/ppermute | solution.py:61
  128.0 10.7 %collective-permute-done.11 = f32[128,1024]{0,1:T(8,128)} collective-permute-done((f32[128,1024]{0,1:T(8,128)S(1)}, f32[128,1024]{0,1:T(8,128)}, u32[]{:S(2)}, u32[]{:S(2)}) %collective-permute-start.11) | collective-permute-done | bytes 524320 | tf_op jit(solution)/shard_map/ppermute | solution.py:61
  138.6 16.4 %collective-permute-done.12 = f32[128,1024]{0,1:T(8,128)} collective-permute-done((f32[128,1024]{0,1:T(8,128)}, f32[128,1024]{0,1:T(8,128)}, u32[]{:S(2)}, u32[]{:S(2)}) %collective-permute-start.12) | collective-permute-done | bytes 524320 | tf_op jit(solution)/shard_map/ppermute | solution.py:61
  157.7 13.2 %collective-permute-done.13 = f32[128,1024]{0,1:T(8,128)} collective-permute-done((f32[128,1024]{0,1:T(8,128)}, f32[128,1024]{0,1:T(8,128)}, u32[]{:S(2)}, u32[]{:S(2)}) %collective-permute-start.13) | collective-permute-done | bytes 524320 | tf_op jit(solution)/shard_map/ppermute | solution.py:61
  181.1 17.8 %fusion.1 = f32[1024,1024]{1,0:T(8,128)} fusion(s32[]{:T(128)S(6)} %select_n.137, f32[1024,1024]{0,1:T(8,128)} %constant_dynamic-update-slice_fusion.8, f32[1024,1024]{0,1:T(8,128)} %all-reduce.7.cloned.1.call-done), kind=kOutput, calls=%fused_computation.5 | convolution fusion | flops 12888047616 | bytes 12582916 | tf_op jit(solution)/shard_map/dot_general | solution.py:20
  198.9 5.4 copy.8
  204.3 20.0 %fusion.23 = f32[1024,1024]{1,0:T(8,128)S(1)} fusion(f32[1024,1024]{1,0:T(8,128)} %fusion.1, f32[1024,1024]{0,1:T(8,128)} %copy.8, f32[2,1024,1024]{2,1,0:T(8,128)} %param.7), kind=kOutput, calls=%fused_computation.25 | convolution fusion | flops 12898533376 | bytes 16777216 | tf_op jit(solution)/shard_map/dot_general | solution.py:20
  224.2 16.8 %fusion.21 = f32[1024,1024]{1,0:T(8,128)} fusion(f32[1024,1024]{1,0:T(8,128)S(1)} %fusion.23, f32[2,1024,1024]{2,1,0:T(8,128)} %param.7), kind=kOutput, calls=%fused_computation.23 | convolution fusion | flops 12884901888 | bytes 12582912 | tf_op jit(solution)/shard_map/dot_general | solution.py:20
  241.1 5.3 copy.9
  246.4 6.5 %select_multiply_fusion.1 = (f32[1024,1024]{0,1:T(8,128)}, f32[1024,1024]{0,1:T(8,128)}) fusion(f32[1024,1024]{0,1:T(8,128)} %copy.9), kind=kLoop, calls=%fused_computation.34 | loop fusion | flops 9437184 | bytes 12582912 | tf_op jit(solution)/shard_map/mul | solution.py:16
  252.9 6.2 %fusion.53 = f32[128,1024]{0,1:T(8,128)S(1)} fusion(f32[1,1024,1024]{1,2,0:T(8,128)} %all-gather.5.cloned.1.call-done, f32[1024,1024]{0,1:T(8,128)} %bitcast.96, s32[]{:T(128)S(6)} %select_n.115, f32[1024,1024]{0,1:T(8,128)} %get-tuple-element.14, f32[1,128,1024]{1,2,0:T(8,128)S(1)} %copy.23, f32[1024,1024]{0,1:T(8,128)} %get-tuple-element.15, ...), kind=kOutput, calls=%fused_computation.60 | convolution fusion | flops 1611399168 | bytes 7473664 | tf_op jit(solution)/shard_map/dot_general | solution.py:20
  262.7 84.1 %all-reduce.11.cloned.1.call-done = (f32[2,128,1024]{1,2,0:T(8,128)}, f32[2,128,1024]{1,2,0:T(8,128)}) async-done(((f32[2,128,1024]{1,2,0:T(8,128)}, f32[2,128,1024]{1,2,0:T(8,128)}), (f32[2,128,1024]{1,2,0:T(8,128)}, f32[2,128,1024]{1,2,0:T(8,128)})) %all-reduce.11.cloned.1.call-update) | async-done | bytes 2097168 | tf_op jit(solution)/shard_map/psum | solution.py:11
  352.8 5.1 convolution_subtract_fusion
  359.2 10.9 %collective-permute-done = f32[128,1024]{0,1:T(8,128)S(1)} collective-permute-done((f32[128,1024]{0,1:T(8,128)S(1)}, f32[128,1024]{0,1:T(8,128)S(1)}, u32[]{:S(2)}, u32[]{:S(2)}) %collective-permute-start) | collective-permute-done | bytes 524320 | tf_op jit(solution)/shard_map/ppermute | solution.py:61
  370.8 19.9 %collective-permute-done.1 = f32[128,1024]{0,1:T(8,128)S(1)} collective-permute-done((f32[128,1024]{0,1:T(8,128)S(1)}, f32[128,1024]{0,1:T(8,128)S(1)}, u32[]{:S(2)}, u32[]{:S(2)}) %collective-permute-start.1) | collective-permute-done | bytes 524320 | tf_op jit(solution)/shard_map/ppermute | solution.py:61
  390.7 5.0 fusion.92
  400.3 20.6 %collective-permute-done.3 = f32[128,1024]{0,1:T(8,128)S(1)} collective-permute-done((f32[128,1024]{0,1:T(8,128)}, f32[128,1024]{0,1:T(8,128)S(1)}, u32[]{:S(2)}, u32[]{:S(2)}) %collective-permute-start.3) | collective-permute-done | bytes 524320 | tf_op jit(solution)/shard_map/ppermute | solution.py:61
  421.0 10.7 %collective-permute-done.4 = f32[128,1024]{0,1:T(8,128)S(1)} collective-permute-done((f32[128,1024]{0,1:T(8,128)S(1)}, f32[128,1024]{0,1:T(8,128)S(1)}, u32[]{:S(2)}, u32[]{:S(2)}) %collective-permute-start.4) | collective-permute-done | bytes 524320 | tf_op jit(solution)/shard_map/ppermute | solution.py:61
  431.6 15.2 %collective-permute-done.5 = f32[128,1024]{0,1:T(8,128)} collective-permute-done((f32[128,1024]{0,1:T(8,128)S(1)}, f32[128,1024]{0,1:T(8,128)}, u32[]{:S(2)}, u32[]{:S(2)}) %collective-permute-start.5) | collective-permute-done | bytes 524320 | tf_op jit(solution)/shard_map/ppermute | solution.py:61
  447.3 8.7 %fusion.68 = f32[1,128,1024]{1,2,0:T(8,128)S(1)} fusion(f32[128,1024]{0,1:T(8,128)S(1)} %copy.16, f32[128,1024]{0,1:T(8,128)S(1)} %fusion.53, f32[128,1024]{1,0:T(8,128)S(1)} %fusion.17, f32[1,1024,1024]{2,1,0:T(8,128)} %all-gather.7.cloned.1.call-done, pred[1024]{0:T(1024)(128)(4,1)S(1)} %fusion.100, pred[]{:T(512)S(6)} %eq.36), kind=kOutput, calls=%fused_computation.65 | convolution fusion | flops 1611005952 | bytes 6292481 | tf_op jit(solution)/shard_map/qib,bj->qij/dot_general | solution.py:83
  456.1 5.1 collective-permute-done.6
  472.5 15.6 %all-reduce.9.cloned.1.call-done = f32[1024,1024]{0,1:T(8,128)} async-done(((f32[1024,1024]{0,1:T(8,128)}), f32[1024,1024]{0,1:T(8,128)}) %all-reduce.9.cloned.1.call-update) | async-done | bytes 4194320 | tf_op jit(solution)/shard_map/psum | solution.py:29
  488.1 17.9 %fusion.4 = f32[1024,1024]{1,0:T(8,128)} fusion(s32[]{:T(128)S(6)} %select_n.137, f32[1024,1024]{0,1:T(8,128)} %constant_dynamic-update-slice_fusion, f32[1024,1024]{0,1:T(8,128)} %all-reduce.9.cloned.1.call-done), kind=kOutput, calls=%fused_computation.7 | convolution fusion | flops 12888047616 | bytes 12582916 | tf_op jit(solution)/shard_map/dot_general | solution.py:20
  506.0 5.4 copy.11
  511.3 20.4 %fusion.12 = f32[1024,1024]{1,0:T(8,128)S(1)} fusion(f32[1024,1024]{1,0:T(8,128)} %fusion.4, f32[1024,1024]{0,1:T(8,128)} %copy.11, f32[2,1024,1024]{2,1,0:T(8,128)} %param.7), kind=kOutput, calls=%fused_computation.15 | convolution fusion | flops 12898533376 | bytes 16777216 | tf_op jit(solution)/shard_map/dot_general | solution.py:20
  531.7 16.8 %fusion.14 = f32[1024,1024]{1,0:T(8,128)} fusion(f32[1024,1024]{1,0:T(8,128)S(1)} %fusion.12, f32[2,1024,1024]{2,1,0:T(8,128)} %param.7), kind=kOutput, calls=%fused_computation.16 | convolution fusion | flops 12884901888 | bytes 12582912 | tf_op jit(solution)/shard_map/dot_general | solution.py:20
  548.6 5.6 copy.12
  558.9 9.7 %fusion.80 = f32[1,128,1024]{1,2,0:T(8,128)S(1)} fusion(f32[128,1024]{0,1:T(8,128)} %reduce-scatter.2.cloned.1.call-done, f32[1,1024,1024]{2,1,0:T(8,128)} %all-gather.7.cloned.1.call-done, f32[1024,1024]{0,1:T(8,128)} %bitcast.95, s32[]{:T(128)S(6)} %select_n.115, f32[1024,1024]{0,1:T(8,128)} %select_multiply_fusion, f32[1,128,1024]{1,2,0:T(8,128)S(1)} %copy.22, ...), kind=kOutput, calls=%fused_computation.69 | convolution fusion | flops 1611530240 | bytes 7997952 | tf_op jit(solution)/shard_map/dot_general | solution.py:20
  (111 shorter events, 58.6 us)
Async XLA Ops:
  6.5 60.0 %all-reduce.13.cloned.1.call-start = ((), (), s32[]{:S(2)}) async-start(), calls=%async_computation.7 | async-start | bytes 2097152 | tf_op jit(solution)/shard_map/psum | solution.py:11
  11.5 169.6 %all-reduce.7.cloned.1.call-start = ((), (), s32[]{:S(2)}) async-start(), calls=%async_computation.1 | async-start | bytes 8388608 | tf_op jit(solution)/shard_map/psum | solution.py:29
  69.9 183.0 %all-gather.5.cloned.1.call-start = ((), (), s32[]{:S(2)}) async-start(), calls=%async_computation.4 | async-start | bytes 4718592 | tf_op jit(solution)/shard_map/all_gather | solution.py:58
  70.0 12.8 %collective-permute-start.7 = (f32[128,1024]{0,1:T(8,128)S(1)}, f32[128,1024]{0,1:T(8,128)S(1)}, u32[]{:S(2)}, u32[]{:S(2)}) collective-permute-start(f32[128,1024]{0,1:T(8,128)S(1)} %copy-done.3), channel_id=1, source_target_pairs={{0,1},{1,2},{2,3},{3,4},{4,5},{5,6},{6,7},{7,0},{8,9},{9,10},{10,1... | collective-permute-start | bytes 1572872 | tf_op jit(solution)/shard_map/ppermute | solution.py:61
  70.6 276.1 %all-reduce.11.cloned.1.call-start = ((), (), s32[]{:S(2)}) async-start(), calls=%async_computation.6 | async-start | bytes 4194304 | tf_op jit(solution)/shard_map/psum | solution.py:11
  82.7 72.4 %copy-start.4 = (f32[128,1024]{0,1:T(8,128)}, f32[128,1024]{0,1:T(8,128)S(1)}, u32[]{:S(2)}) copy-start(f32[128,1024]{0,1:T(8,128)S(1)} %collective-permute-done.7) | copy-start | bytes 1572868
  82.7 19.3 %collective-permute-start.8 = (f32[128,1024]{0,1:T(8,128)S(1)}, f32[128,1024]{0,1:T(8,128)S(1)}, u32[]{:S(2)}, u32[]{:S(2)}) collective-permute-start(f32[128,1024]{0,1:T(8,128)S(1)} %collective-permute-done.7), channel_id=1, source_target_pairs={{0,1},{1,2},{2,3},{3,4},{4,5},{5,6},{6,7},{7,0},{8,9},{9,10},{10,1... | collective-permute-start | bytes 1572872 | tf_op jit(solution)/shard_map/ppermute | solution.py:61
  102.8 14.0 %collective-permute-start.9 = (f32[128,1024]{0,1:T(8,128)S(1)}, f32[128,1024]{0,1:T(8,128)S(1)}, u32[]{:S(2)}, u32[]{:S(2)}) collective-permute-start(f32[128,1024]{0,1:T(8,128)S(1)} %collective-permute-done.8), channel_id=1, source_target_pairs={{0,1},{1,2},{2,3},{3,4},{4,5},{5,6},{6,7},{7,0},{8,9},{9,10},{10,1... | collective-permute-start | bytes 1572872 | tf_op jit(solution)/shard_map/ppermute | solution.py:61
  117.6 9.6 %collective-permute-start.10 = (f32[128,1024]{0,1:T(8,128)S(1)}, f32[128,1024]{0,1:T(8,128)S(1)}, u32[]{:S(2)}, u32[]{:S(2)}) collective-permute-start(f32[128,1024]{0,1:T(8,128)S(1)} %collective-permute-done.9), channel_id=1, source_target_pairs={{0,1},{1,2},{2,3},{3,4},{4,5},{5,6},{6,7},{7,0},{8,9},{9,10},{10,1... | collective-permute-start | bytes 1572872 | tf_op jit(solution)/shard_map/ppermute | solution.py:61
  128.0 10.7 %collective-permute-start.11 = (f32[128,1024]{0,1:T(8,128)S(1)}, f32[128,1024]{0,1:T(8,128)}, u32[]{:S(2)}, u32[]{:S(2)}) collective-permute-start(f32[128,1024]{0,1:T(8,128)S(1)} %collective-permute-done.10), channel_id=1, source_target_pairs={{0,1},{1,2},{2,3},{3,4},{4,5},{5,6},{6,7},{7,0},{8,9},{9,10},{10,1... | collective-permute-start | bytes 1572872 | tf_op jit(solution)/shard_map/ppermute | solution.py:61
  138.6 16.4 %collective-permute-start.12 = (f32[128,1024]{0,1:T(8,128)}, f32[128,1024]{0,1:T(8,128)}, u32[]{:S(2)}, u32[]{:S(2)}) collective-permute-start(f32[128,1024]{0,1:T(8,128)} %collective-permute-done.11), channel_id=1, source_target_pairs={{0,1},{1,2},{2,3},{3,4},{4,5},{5,6},{6,7},{7,0},{8,9},{9,10},{10,1... | collective-permute-start | bytes 1572872 | tf_op jit(solution)/shard_map/ppermute | solution.py:61
  155.1 15.9 %collective-permute-start.13 = (f32[128,1024]{0,1:T(8,128)}, f32[128,1024]{0,1:T(8,128)}, u32[]{:S(2)}, u32[]{:S(2)}) collective-permute-start(f32[128,1024]{0,1:T(8,128)} %collective-permute-done.12), channel_id=1, source_target_pairs={{0,1},{1,2},{2,3},{3,4},{4,5},{5,6},{6,7},{7,0},{8,9},{9,10},{10,1... | collective-permute-start | bytes 1572872 | tf_op jit(solution)/shard_map/ppermute | solution.py:61
  155.3 21.3 %copy-start.13 = (f32[128,1024]{0,1:T(8,128)S(1)}, f32[128,1024]{0,1:T(8,128)}, u32[]{:S(2)}) copy-start(f32[128,1024]{0,1:T(8,128)} %copy-done.12) | copy-start | bytes 1572868
  155.3 22.2 %copy-start.9 = (f32[128,1024]{0,1:T(8,128)S(1)}, f32[128,1024]{0,1:T(8,128)}, u32[]{:S(2)}) copy-start(f32[128,1024]{0,1:T(8,128)} %copy-done.8) | copy-start | bytes 1572868
  155.3 23.1 %copy-start.7 = (f32[128,1024]{0,1:T(8,128)S(1)}, f32[128,1024]{0,1:T(8,128)}, u32[]{:S(2)}) copy-start(f32[128,1024]{0,1:T(8,128)} %copy-done.6) | copy-start | bytes 1572868
  156.6 22.7 %copy-start.5 = (f32[128,1024]{0,1:T(8,128)S(1)}, f32[128,1024]{0,1:T(8,128)}, u32[]{:S(2)}) copy-start(f32[128,1024]{0,1:T(8,128)} %copy-done.4) | copy-start | bytes 1572868
  260.2 187.0 %all-gather.7.cloned.1.call-start = ((), (), s32[]{:S(2)}) async-start(), calls=%async_computation.5 | async-start | bytes 4718592 | tf_op jit(solution)/shard_map/all_gather | solution.py:58
  262.2 225.9 %all-reduce.9.cloned.1.call-start = ((), (), s32[]{:S(2)}) async-start(), calls=%async_computation.2 | async-start | bytes 8388608 | tf_op jit(solution)/shard_map/psum | solution.py:29
  358.0 200.9 %reduce-scatter.2.cloned.1.call-start = ((), (), s32[]{:S(2)}) async-start(), calls=%async_computation.3 | async-start | bytes 4718592 | tf_op jit(solution)/shard_map/reduce_scatter | solution.py:75
  359.1 10.9 %collective-permute-start = (f32[128,1024]{0,1:T(8,128)S(1)}, f32[128,1024]{0,1:T(8,128)S(1)}, u32[]{:S(2)}, u32[]{:S(2)}) collective-permute-start(f32[128,1024]{0,1:T(8,128)S(1)} %slice_bitcast_fusion.5), channel_id=1, source_target_pairs={{0,1},{1,2},{2,3},{3,4},{4,5},{5,6},{6,7},{7,0},{8,9},{9,10},{10,1... | collective-permute-start | bytes 1572872 | tf_op jit(solution)/shard_map/ppermute | solution.py:61
  370.8 19.9 %collective-permute-start.1 = (f32[128,1024]{0,1:T(8,128)S(1)}, f32[128,1024]{0,1:T(8,128)S(1)}, u32[]{:S(2)}, u32[]{:S(2)}) collective-permute-start(f32[128,1024]{0,1:T(8,128)S(1)} %collective-permute-done), channel_id=1, source_target_pairs={{0,1},{1,2},{2,3},{3,4},{4,5},{5,6},{6,7},{7,0},{8,9},{9,10},{10,1... | collective-permute-start | bytes 1572872 | tf_op jit(solution)/shard_map/ppermute | solution.py:61
  390.7 9.6 %collective-permute-start.2 = (f32[128,1024]{0,1:T(8,128)S(1)}, f32[128,1024]{0,1:T(8,128)}, u32[]{:S(2)}, u32[]{:S(2)}) collective-permute-start(f32[128,1024]{0,1:T(8,128)S(1)} %collective-permute-done.1), channel_id=1, source_target_pairs={{0,1},{1,2},{2,3},{3,4},{4,5},{5,6},{6,7},{7,0},{8,9},{9,10},{10,1... | collective-permute-start | bytes 1572872 | tf_op jit(solution)/shard_map/ppermute | solution.py:61
  400.3 20.6 %collective-permute-start.3 = (f32[128,1024]{0,1:T(8,128)}, f32[128,1024]{0,1:T(8,128)S(1)}, u32[]{:S(2)}, u32[]{:S(2)}) collective-permute-start(f32[128,1024]{0,1:T(8,128)} %collective-permute-done.2), channel_id=1, source_target_pairs={{0,1},{1,2},{2,3},{3,4},{4,5},{5,6},{6,7},{7,0},{8,9},{9,10},{10,1... | collective-permute-start | bytes 1572872 | tf_op jit(solution)/shard_map/ppermute | solution.py:61
  421.0 26.1 %copy-start.16 = (f32[128,1024]{0,1:T(8,128)}, f32[128,1024]{0,1:T(8,128)S(1)}, u32[]{:S(2)}) copy-start(f32[128,1024]{0,1:T(8,128)S(1)} %collective-permute-done.3) | copy-start | bytes 1572868
  421.0 10.7 %collective-permute-start.4 = (f32[128,1024]{0,1:T(8,128)S(1)}, f32[128,1024]{0,1:T(8,128)S(1)}, u32[]{:S(2)}, u32[]{:S(2)}) collective-permute-start(f32[128,1024]{0,1:T(8,128)S(1)} %collective-permute-done.3), channel_id=1, source_target_pairs={{0,1},{1,2},{2,3},{3,4},{4,5},{5,6},{6,7},{7,0},{8,9},{9,10},{10,1... | collective-permute-start | bytes 1572872 | tf_op jit(solution)/shard_map/ppermute | solution.py:61
  431.6 15.7 %copy-start.18 = (f32[128,1024]{0,1:T(8,128)}, f32[128,1024]{0,1:T(8,128)S(1)}, u32[]{:S(2)}) copy-start(f32[128,1024]{0,1:T(8,128)S(1)} %collective-permute-done.4) | copy-start | bytes 1572868
  431.6 15.2 %collective-permute-start.5 = (f32[128,1024]{0,1:T(8,128)S(1)}, f32[128,1024]{0,1:T(8,128)}, u32[]{:S(2)}, u32[]{:S(2)}) collective-permute-start(f32[128,1024]{0,1:T(8,128)S(1)} %collective-permute-done.4), channel_id=1, source_target_pairs={{0,1},{1,2},{2,3},{3,4},{4,5},{5,6},{6,7},{7,0},{8,9},{9,10},{10,1... | collective-permute-start | bytes 1572872 | tf_op jit(solution)/shard_map/ppermute | solution.py:61
  446.8 14.4 %collective-permute-start.6 = (f32[128,1024]{0,1:T(8,128)}, f32[128,1024]{0,1:T(8,128)}, u32[]{:S(2)}, u32[]{:S(2)}) collective-permute-start(f32[128,1024]{0,1:T(8,128)} %collective-permute-done.5), channel_id=1, source_target_pairs={{0,1},{1,2},{2,3},{3,4},{4,5},{5,6},{6,7},{7,0},{8,9},{9,10},{10,1... | collective-permute-start | bytes 1572872 | tf_op jit(solution)/shard_map/ppermute | solution.py:61
  447.3 19.7 %copy-start.17 = (f32[128,1024]{0,1:T(8,128)S(1)}, f32[128,1024]{0,1:T(8,128)}, u32[]{:S(2)}) copy-start(f32[128,1024]{0,1:T(8,128)} %copy-done.16) | copy-start | bytes 1572868
  456.0 13.9 %copy-start.15 = (f32[128,1024]{0,1:T(8,128)S(1)}, f32[128,1024]{0,1:T(8,128)}, u32[]{:S(2)}) copy-start(f32[128,1024]{0,1:T(8,128)} %copy-done.14) | copy-start | bytes 1572868
  456.0 14.7 %copy-start.11 = (f32[128,1024]{0,1:T(8,128)S(1)}, f32[128,1024]{0,1:T(8,128)}, u32[]{:S(2)}) copy-start(f32[128,1024]{0,1:T(8,128)} %copy-done.10) | copy-start | bytes 1572868
  456.0 15.6 %copy-start.1 = (f32[2,128,1024]{1,2,0:T(8,128)S(1)}, f32[2,128,1024]{1,2,0:T(8,128)}, u32[]{:S(2)}) copy-start(f32[2,128,1024]{1,2,0:T(8,128)} %get-tuple-element.7) | copy-start | bytes 3145732
  (9 other events, 20.3 us)
Sparse Core Ops, SparseCore 0:
  11.6 54.8 all-reduce.12
  70.1 98.5 all-reduce.6
  170.6 36.5 all-gather.4
  260.3 86.3 all-reduce.10
  348.7 42.5 all-gather.6
  394.7 93.3 all-reduce.8
  491.5 51.3 reduce-scatter.1
